TPU v7x, 32 devices: a whole 2x2x4 slice. The times are simulated.
32 devices in a mesh: seq: 8 (over z, x), win: 4 (over y, core).
Axes of the slice: x: 2, y: 2, z: 4, core: 2. Of those that a mesh axis runs over, the one named last changes fastest.
Arguments:
- inputs: bfloat16 [4, 3072, 1536], P('win', 'seq'), may hold values from -6 to 6
- cotangent: bfloat16 [4, 3072, 1536], P('win', 'seq'), may hold values from -6 to 6
- w_dilated: bfloat16 [2, 1536, 3, 768], P(None, ('seq', 'win')), may hold values from -0.09375 to 0.09375
- w_mix: bfloat16 [2, 1536, 768], P(None, ('seq', 'win')), may hold values from -0.21875 to 0.21875
- in_scale: float32 [2, 1536], replicated, may hold values from 0.1 to 1.9
- in_shift: float32 [2, 1536], replicated, may hold values from -3 to 3
- mid_scale: float32 [2, 768], replicated, may hold values from 0.1 to 1.9
- mid_shift: float32 [2, 768], replicated, may hold values from -3 to 3
Outputs:
- output: bfloat16 [4, 3072, 1536], P('win', 'seq')
- input_gradient: float32 [4, 3072, 1536], P('win', 'seq')
- dilated_weight_gradient: float32 [2, 1536, 3, 768], P(None, ('seq', 'win'))
- grad_mix: float32 [2, 1536, 768], P(None, ('seq', 'win'))
All inputs are finite; a program needn't handle non-finite values.
Results may differ from a plain program's by a relative error of at most 0.034.
Values may be sent and summed in bfloat16 or wider, within the bound.
No kernel may reach another device: no remote copies, remote signals or barrier semaphores. Data moves between devices by JAX's collectives and lax.ppermute only.
A program may use at most 192 MiB of HBM per device.

v0:
```python
import math
import jax
import jax.numpy as jnp
from jax import lax
from jax.sharding import PartitionSpec as P

dilation_steps = (8, 16)


def padded_2(block, sides, width):
    for axis, dim in sides:
        count = lax.axis_size(axis)
        forward = [(i, i + 1) for i in range(count - 1)]
        backward = [(target, source) for source, target in forward]
        low = lax.ppermute(
            lax.slice_in_dim(block, block.shape[dim] - width, None, axis=dim), axis, forward
        )
        high = lax.ppermute(lax.slice_in_dim(block, 0, width, axis=dim), axis, backward)
        block = jnp.concatenate([low, block, high], axis=dim)
    return block


def gelu_value(values):
    return jax.nn.gelu(values, approximate=True)


def gelu_back(pre_values, upstream_gradient):
    return jax.vjp(gelu_value, pre_values)[1](upstream_gradient)[0]


def dilated_conv(padded, w_conv, dilation, out_rows):
    hidden = jnp.dot(padded[0:out_rows], w_conv[:, 0, :], preferred_element_type=jnp.float32)
    for kernel_tap in (1, 2):
        lower = kernel_tap * dilation
        hidden = hidden + jnp.dot(
            padded[lower : lower + out_rows],
            w_conv[:, kernel_tap, :],
            preferred_element_type=jnp.float32,
        )
    return hidden


def fetch_weights(w_dilated, w_mix):
    blocks, rows, taps, c2 = w_dilated.shape
    local = jnp.concatenate(
        [
            w_dilated.reshape(blocks, rows, taps * c2).transpose(1, 0, 2).reshape(rows, -1),
            w_mix.transpose(1, 0, 2).reshape(rows, -1),
        ],
        axis=1,
    )
    gathered = lax.all_gather(local, ("seq", "win"), axis=0, tiled=True)
    full_rows = gathered.shape[0]
    split = blocks * taps * c2
    return [
        (
            gathered[:, b * taps * c2 : (b + 1) * taps * c2].reshape(full_rows, taps, c2),
            gathered[:, split + b * c2 : split + (b + 1) * c2],
        )
        for b in range(blocks)
    ]


def weight_gradient_terms(padded, d_hidden, cot_here, middle, dilation, inverse_square_root):
    row_count = d_hidden.shape[0]
    kernel_taps = [
        jnp.einsum(
            "pc,pe->ce",
            padded[kernel_tap * dilation : kernel_tap * dilation + row_count],
            d_hidden,
            preferred_element_type=jnp.float32,
        )
        for kernel_tap in range(3)
    ]
    dilated = (jnp.concatenate(kernel_taps, axis=1) * inverse_square_root).astype(jnp.bfloat16)
    mixed = (
        jnp.einsum("pc,pe->ce", cot_here, middle, preferred_element_type=jnp.float32)
        * inverse_square_root
    ).astype(jnp.bfloat16)
    return (dilated, mixed)


def per_device(inputs, cotangent, w_dilated, w_mix, in_scale, in_shift, mid_scale, mid_shift):
    x_local = inputs[0]
    cot_local = cotangent[0]
    row_count = x_local.shape[0]
    window_len = lax.axis_size("seq") * row_count
    inverse_square_root = 1.0 / math.sqrt(lax.axis_size("win") * inputs.shape[0] * window_len)
    residual_block_count = len(dilation_steps)
    saved = []
    weights = fetch_weights(w_dilated, w_mix)
    stream = x_local.astype(jnp.float32)
    for residual_block_index in range(residual_block_count):
        dilation = dilation_steps[residual_block_index]
        w_conv, w_out = weights[residual_block_index]
        pre_in = stream * in_scale[residual_block_index] + in_shift[residual_block_index]
        activated = gelu_value(pre_in).astype(jnp.bfloat16)
        padded = padded_2(activated, (("seq", 0),), dilation)
        pre_mid = (
            dilated_conv(padded, w_conv, dilation, row_count) * mid_scale[residual_block_index]
            + mid_shift[residual_block_index]
        )
        middle = gelu_value(pre_mid).astype(jnp.bfloat16)
        stream = stream + jnp.einsum("pe,ce->pc", middle, w_out, preferred_element_type=jnp.float32)
        saved.append((w_conv, w_out, pre_in, padded, pre_mid, middle))
    output = stream.astype(jnp.bfloat16)
    upstream_gradient = cot_local.astype(jnp.float32)
    dilated_weight_gradients = [None] * residual_block_count
    mixing_weight_gradients = [None] * residual_block_count
    for residual_block_index in reversed(range(residual_block_count)):
        dilation = dilation_steps[residual_block_index]
        w_conv, w_out, pre_in, padded, pre_mid, middle = saved[residual_block_index]
        cot_here = upstream_gradient.astype(jnp.bfloat16)
        d_mid = jnp.dot(cot_here, w_out, preferred_element_type=jnp.float32)
        d_hidden = (gelu_back(pre_mid, d_mid) * mid_scale[residual_block_index]).astype(
            jnp.bfloat16
        )
        d_pad = padded_2(d_hidden, (("seq", 0),), dilation)
        d_act = jnp.einsum(
            "pe,ce->pc",
            d_pad[2 * dilation : 2 * dilation + row_count],
            w_conv[:, 0, :],
            preferred_element_type=jnp.float32,
        )
        for kernel_tap in (1, 2):
            lower = (2 - kernel_tap) * dilation
            d_act = d_act + jnp.einsum(
                "pe,ce->pc",
                d_pad[lower : lower + row_count],
                w_conv[:, kernel_tap, :],
                preferred_element_type=jnp.float32,
            )
        (
            dilated_weight_gradients[residual_block_index],
            mixing_weight_gradients[residual_block_index],
        ) = weight_gradient_terms(padded, d_hidden, cot_here, middle, dilation, inverse_square_root)
        upstream_gradient = (
            upstream_gradient + gelu_back(pre_in, d_act) * in_scale[residual_block_index]
        )
    summed = lax.psum_scatter(
        jnp.concatenate(dilated_weight_gradients + mixing_weight_gradients, axis=1),
        ("seq", "win"),
        scatter_dimension=0,
        tiled=True,
    ).astype(jnp.float32)
    own_rows = summed.shape[0]
    taps, c2 = (w_dilated.shape[2], w_dilated.shape[3])
    split = residual_block_count * taps * c2
    return (
        output[None],
        upstream_gradient[None],
        summed[:, :split].reshape(own_rows, residual_block_count, taps, c2).transpose(1, 0, 2, 3),
        summed[:, split:].reshape(own_rows, residual_block_count, c2).transpose(1, 0, 2),
    )


def solution(mesh):
    in_specs = (
        P("win", "seq", None),
        P("win", "seq", None),
        P(None, ("seq", "win"), None, None),
        P(None, ("seq", "win"), None),
        P(),
        P(),
        P(),
        P(),
    )
    out_specs = (
        P("win", "seq", None),
        P("win", "seq", None),
        P(None, ("seq", "win"), None, None),
        P(None, ("seq", "win"), None),
    )
    return jax.shard_map(
        per_device, mesh=mesh, in_specs=in_specs, out_specs=out_specs, check_vma=False
    )
```

profile of v0, /device:TPU:0, one launch (start us, length us, event | category | flops | bytes accessed | tf_op | source)
XLA Modules:
  0.0 499.8 jit_solution(18363902650150961037)
XLA Ops:
  7.2 1.0 copy.44
  8.3 1.0 copy.42
  11.4 1.3 collective-permute-start.1
  12.7 5.5 %collective-permute-start = (bf16[8,1536]{1,0:T(8,128)(2,1)S(1)}, bf16[8,1536]{1,0:T(8,128)(2,1)S(1)}, u32[]{:S(2)}, u32[]{:S(2)}) collective-permute-start(bf16[8,1536]{1,0:T(8,128)(2,1)S(1)} %get-tuple-element.16), channel_id=1, source_target_pairs={{0,4},{4,8},{8,12},{12,16},{16,20},{20,24},{24,28},{1,5},{5,9},{9,... | collective-permute-start | bytes 73736 | tf_op jit(solution)/shard_map/ppermute | solution.py:15
  18.2 120.7 %all-gather.2.cloned.1.call-done = bf16[1536,6144]{1,0:T(8,128)(2,1)} async-done(((bf16[48,6144]{1,0:T(8,128)(2,1)}), bf16[1536,6144]{1,0:T(8,128)(2,1)}) %all-gather.2.cloned.1.call-update) | async-done | bytes 18874384 | tf_op jit(solution)/shard_map/all_gather | solution.py:52
  138.9 10.1 %fusion.125 = (bf16[1536,2304]{1,0:T(8,128)(2,1)}, bf16[1536,2304]{1,0:T(8,128)(2,1)}) fusion(bf16[1536,6144]{1,0:T(8,128)(2,1)} %all-gather.2.cloned.1.call-done), kind=kLoop, calls=%fused_computation.163 | loop fusion | bytes 28311552 | tf_op jit(solution)/shard_map/slice | solution.py:57
  149.0 10.2 %copy.30 = bf16[1536,2304]{0,1:T(8,128)(2,1)} copy(bf16[1536,2304]{1,0:T(8,128)(2,1)} %get-tuple-element.13) | data formatting | bytes 14155776 | tf_op jit(solution)/shard_map/slice | solution.py:57
  159.2 4.4 fusion.42
  163.6 3.8 fusion.44
  167.4 10.3 %copy.34 = bf16[1536,2304]{0,1:T(8,128)(2,1)} copy(bf16[1536,2304]{1,0:T(8,128)(2,1)} %get-tuple-element.12) | data formatting | bytes 14155776 | tf_op jit(solution)/shard_map/slice | solution.py:57
  177.7 3.6 fusion.66
  181.3 3.6 multiply_convert_fusion.2
  185.0 1.3 collective-permute-start.3
  186.3 1.1 fusion.47
  187.4 4.7 collective-permute-start.2
  192.2 1.1 fusion.49
  193.7 1.1 fusion.62
  195.0 3.0 fusion.2
  197.9 3.3 fusion.82
  201.2 1.5 fusion.131
  202.7 4.2 collective-permute-start.5
  206.9 1.5 fusion.102
  208.4 1.5 fusion.101
  209.9 4.3 fusion.1
  214.2 1.1 fusion.46
  215.3 1.5 collective-permute-start.4
  216.8 1.1 fusion.48
  217.9 4.3 collective-permute-done.4
  222.2 2.7 fusion.38
  224.9 2.9 multiply_convert_fusion.1
  227.9 3.3 fusion.74
  231.1 1.5 fusion.130
  232.6 1.4 fusion.100
  234.0 1.5 fusion.99
  235.5 4.3 fusion
  239.7 17.0 %pad_maximum_fusion = bf16[1536,6144]{0,1:T(8,128)(2,1)} fusion(bf16[1536,768]{0,1:T(8,128)(2,1)} %fusion.2, bf16[1536,768]{0,1:T(8,128)(2,1)} %multiply_convert_fusion.1, bf16[1536,2304]{0,1:T(8,128)(2,1)} %fusion.1, bf16[1536,2304]{0,1:T(8,128)(2,1)} %fusion), kind=kLoop, calls=%fused_computation | loop fusion | flops 75497472 | bytes 37748736 | tf_op jit(solution)/shard_map/concatenate | solution.py:141
  256.7 24.7 %copy.40 = bf16[1536,6144]{1,0:T(8,128)(2,1)} copy(bf16[1536,6144]{0,1:T(8,128)(2,1)} %pad_maximum_fusion) | data formatting | bytes 37748736
  281.5 1.2 copy-done.11
  282.7 4.6 fusion.7
  287.3 5.1 %collective-permute-start.7 = (bf16[8,768]{1,0:T(8,128)(2,1)S(1)}, bf16[8,768]{1,0:T(8,128)(2,1)S(1)}, u32[]{:S(2)}, u32[]{:S(2)}) collective-permute-start(bf16[8,768]{1,0:T(8,128)(2,1)S(1)} %get-tuple-element.19), channel_id=1, source_target_pairs={{0,4},{4,8},{8,12},{12,16},{16,20},{20,24},{24,28},{1,5},{5,9},{9,... | collective-permute-start | bytes 36872 | tf_op jit(solution)/shard_map/ppermute | solution.py:15
  292.4 2.9 fusion.41
  295.3 1.6 collective-permute-start.6
  296.9 2.9 fusion.43
  299.8 1.4 collective-permute-done.6
  301.2 5.9 %fusion.30 = f32[1,384,1536]{2,1,0:T(8,128)} fusion(f32[384,1536]{1,0:T(8,128)S(1)} %copy-done.8, bf16[1,384,1536]{2,1,0:T(8,128)(2,1)S(1)} %copy-done.1, f32[384,1536]{1,0:T(8,128)S(1)} %fusion.43, f32[384,1536]{1,0:T(8,128)S(1)} %fusion.41, bf16[1536,3,768]{0,2,1:T(8,128)(2,1)} %bitcast.154, f32[1536]{0:T(1024)S(1)} %get-tuple-element.7, ...), kind=kOutput, calls=%fused_computation.46 | convolution fusion | flops 922484736 | bytes 13590528 | tf_op jit(solution)/shard_map/pe,ce->pc/dot_general | solution.py:119
  307.1 180.9 %reduce-scatter.4.cloned.1.call-done = bf16[48,6144]{1,0:T(8,128)(2,1)} async-done(((bf16[1536,6144]{1,0:T(8,128)(2,1)}), bf16[48,6144]{1,0:T(8,128)(2,1)}) %reduce-scatter.4.cloned.1.call-update) | async-done | bytes 589840
  488.1 1.1 slice.184
  490.0 1.6 copy.38
  (51 shorter events, 4.8 us)
Async XLA Ops:
  7.2 3.1 copy-start.2
  7.2 3.1 copy-start.3
  7.2 3.2 copy-start.1
  7.2 131.7 %all-gather.2.cloned.1.call-start = ((), (), s32[]{:S(2)}) async-start(), calls=%async_computation.1 | async-start | bytes 19464192 | tf_op jit(solution)/shard_map/all_gather | solution.py:52
  9.3 8.8 %copy-start.4 = (f32[2,768]{1,0:T(2,128)S(1)}, f32[2,768]{1,0:T(2,128)}, u32[]{:S(2)}) copy-start(f32[2,768]{1,0:T(2,128)} %param.15) | copy-start | bytes 18436
  9.4 8.8 %copy-start.5 = (f32[2,768]{1,0:T(2,128)S(1)}, f32[2,768]{1,0:T(2,128)}, u32[]{:S(2)}) copy-start(f32[2,768]{1,0:T(2,128)} %param.14) | copy-start | bytes 18436
  10.2 477.8 %reduce-scatter.4.cloned.1.call-start = ((), (), s32[]{:S(2)}) async-start(), calls=%async_computation.2 | async-start | bytes 19464192
  11.4 152.2 %collective-permute-start.1 = (bf16[8,1536]{1,0:T(8,128)(2,1)S(1)}, bf16[8,1536]{1,0:T(8,128)(2,1)S(1)}, u32[]{:S(2)}, u32[]{:S(2)}) collective-permute-start(bf16[8,1536]{1,0:T(8,128)(2,1)S(1)} %get-tuple-element.17), channel_id=1, source_target_pairs={{4,0},{8,4},{12,8},{16,12},{20,16},{24,20},{28,24},{5,1},{9,5},{13... | collective-permute-start | bytes 73736 | tf_op jit(solution)/shard_map/ppermute | solution.py:18
  12.7 165.0 %collective-permute-start = (bf16[8,1536]{1,0:T(8,128)(2,1)S(1)}, bf16[8,1536]{1,0:T(8,128)(2,1)S(1)}, u32[]{:S(2)}, u32[]{:S(2)}) collective-permute-start(bf16[8,1536]{1,0:T(8,128)(2,1)S(1)} %get-tuple-element.16), channel_id=1, source_target_pairs={{0,4},{4,8},{8,12},{12,16},{16,20},{20,24},{24,28},{1,5},{5,9},{9,... | collective-permute-start | bytes 73736 | tf_op jit(solution)/shard_map/ppermute | solution.py:15
  177.7 8.6 %slice-start = ((s8[7077888]{0:T(1024)(128)(4,1)}), s8[4194304]{0:T(1024)(128)(4,1)S(1)}, s32[]{:S(2)}) async-start(s8[7077888]{0:T(1024)(128)(4,1)} %bitcast.155), calls=%async_computation.3 | async-start | bytes 8388608
  181.3 5.0 slice-start.1
  185.0 37.3 %copy-start.9 = (f32[384,1536]{1,0:T(8,128)}, f32[384,1536]{1,0:T(8,128)S(1)}, u32[]{:S(2)}) copy-start(f32[384,1536]{1,0:T(8,128)S(1)} %get-tuple-element.23) | copy-start | bytes 7077892
  185.0 7.2 %collective-permute-start.3 = (bf16[16,1536]{1,0:T(8,128)(2,1)S(1)}, bf16[16,1536]{1,0:T(8,128)(2,1)S(1)}, u32[]{:S(2)}, u32[]{:S(2)}) collective-permute-start(bf16[16,1536]{1,0:T(8,128)(2,1)S(1)} %get-tuple-element.15), channel_id=1, source_target_pairs={{4,0},{8,4},{12,8},{16,12},{20,16},{24,20},{28,24},{5,1},{9,5},{13... | collective-permute-start | bytes 147464 | tf_op jit(solution)/shard_map/ppermute | solution.py:18
  187.4 6.3 %collective-permute-start.2 = (bf16[16,1536]{1,0:T(8,128)(2,1)S(1)}, bf16[16,1536]{1,0:T(8,128)(2,1)S(1)}, u32[]{:S(2)}, u32[]{:S(2)}) collective-permute-start(bf16[16,1536]{1,0:T(8,128)(2,1)S(1)} %get-tuple-element.14), channel_id=1, source_target_pairs={{0,4},{4,8},{8,12},{12,16},{16,20},{20,24},{24,28},{1,5},{5,9},{9,... | collective-permute-start | bytes 147464 | tf_op jit(solution)/shard_map/ppermute | solution.py:15
  193.7 1.3 copy-start.6
  195.0 3.0 copy-start.10
  202.7 14.1 %collective-permute-start.5 = (bf16[16,768]{1,0:T(8,128)(2,1)S(1)}, bf16[16,768]{1,0:T(8,128)(2,1)S(1)}, u32[]{:S(2)}, u32[]{:S(2)}) collective-permute-start(bf16[16,768]{1,0:T(8,128)(2,1)S(1)} %get-tuple-element.21), channel_id=1, source_target_pairs={{0,4},{4,8},{8,12},{12,16},{16,20},{20,24},{24,28},{1,5},{5,9},{9,... | collective-permute-start | bytes 73736 | tf_op jit(solution)/shard_map/ppermute | solution.py:15
  215.3 6.9 %collective-permute-start.4 = (bf16[16,768]{1,0:T(8,128)(2,1)S(1)}, bf16[16,768]{1,0:T(8,128)(2,1)S(1)}, u32[]{:S(2)}, u32[]{:S(2)}) collective-permute-start(bf16[16,768]{1,0:T(8,128)(2,1)S(1)} %get-tuple-element.20), channel_id=1, source_target_pairs={{4,0},{8,4},{12,8},{16,12},{20,16},{24,20},{28,24},{5,1},{9,5},{13... | collective-permute-start | bytes 73736 | tf_op jit(solution)/shard_map/ppermute | solution.py:18
  224.9 2.9 copy-start.7
  281.5 1.3 copy-start.11
  287.3 9.6 %collective-permute-start.7 = (bf16[8,768]{1,0:T(8,128)(2,1)S(1)}, bf16[8,768]{1,0:T(8,128)(2,1)S(1)}, u32[]{:S(2)}, u32[]{:S(2)}) collective-permute-start(bf16[8,768]{1,0:T(8,128)(2,1)S(1)} %get-tuple-element.19), channel_id=1, source_target_pairs={{0,4},{4,8},{8,12},{12,16},{16,20},{20,24},{24,28},{1,5},{5,9},{9,... | collective-permute-start | bytes 36872 | tf_op jit(solution)/shard_map/ppermute | solution.py:15
  295.3 5.9 %copy-start.8 = (f32[384,1536]{1,0:T(8,128)S(1)}, f32[384,1536]{1,0:T(8,128)}, u32[]{:S(2)}) copy-start(f32[384,1536]{1,0:T(8,128)} %copy-done.7) | copy-start | bytes 7077892
  295.3 5.9 %collective-permute-start.6 = (bf16[8,768]{1,0:T(8,128)(2,1)S(1)}, bf16[8,768]{1,0:T(8,128)(2,1)S(1)}, u32[]{:S(2)}, u32[]{:S(2)}) collective-permute-start(bf16[8,768]{1,0:T(8,128)(2,1)S(1)} %get-tuple-element.18), channel_id=1, source_target_pairs={{4,0},{8,4},{12,8},{16,12},{20,16},{24,20},{28,24},{5,1},{9,5},{13... | collective-permute-start | bytes 36872 | tf_op jit(solution)/shard_map/ppermute | solution.py:18
  490.0 1.7 copy-start
Sparse Core Ops, SparseCore 0:
  11.5 127.3 all-gather.1
  281.6 206.4 reduce-scatter.3
where the time goes:
time: 502 us; the launch traced here: 500 us
  waiting for transfers between devices  308 us (61%)
  local copies, waits for them, and re-layouts  63.7 us (13%)
  matrix products  61.1 us (12%)
  other arithmetic  27.4 us (5%)
  starting transfers between devices  25.2 us (5%)
  between operations  14.5 us (3%)
    unnamed x3, waiting for transfers between devices  181 us
    all_gather x1, waiting for transfers between devices, fetch_weights(): gathered = lax.all_gather(local, ('seq', 'win'), axis=0, tiled=True)  121 us
    slice x3, local copies, waits for them, and re-layouts, fetch_weights(): gathered[:, b * taps * c2:(b + 1) * taps * c2].reshape(full_rows, taps, c2)  30.6 us
    unnamed x31, local copies, waits for them, and re-layouts  27.3 us
    ppermute x4, starting transfers between devices, padded_2(): lax.ppermute(lax.slice_in_dim(block, block.shape[dim] - width, None, axis...  19.5 us
    concatenate x1, other arithmetic, per_device(): jnp.concatenate(dilated_weight_gradients + mixing_weight_gradients, axis=1)  17 us
    dot_general x4, matrix products, dilated_conv(): jnp.dot(padded[lower:lower + out_rows], w_conv[:, kernel_tap, :], preferr...  10.4 us
  transfers between devices with their start and end apart: 10, of which 5 were waited for; matrix products, arithmetic and copies ran while one was open for 14% of the time, Pallas kernels for 0%

commit v1 on v0

--- a/solution.py
+++ b/solution.py
@@ -5,6 +5,28 @@
 from jax.sharding import PartitionSpec as P
 
 dilation_steps = (8, 16)
+
+
+def laid_out(blocks, dim):
+    blocks = jnp.moveaxis(blocks, 0, dim)
+    shape = blocks.shape
+    return blocks.reshape(*shape[:dim], shape[dim] * shape[dim + 1], *shape[dim + 2 :])
+
+
+def doubled(value, axis):
+    length = lax.axis_size(axis)
+    tiles = value[None]
+    for level in range(length.bit_length() - 1):
+        stride = 1 << level
+        other = lax.ppermute(tiles, axis, [(i, i ^ stride) for i in range(length)])
+        both = jnp.stack([tiles, other])
+        upper = lax.axis_index(axis) >> level & 1
+        tiles = jnp.where(upper == 0, both, both[::-1]).reshape(-1, *value.shape)
+    return tiles
+
+
+def gather_by_bits(x, axis, dim):
+    return laid_out(doubled(x, axis), dim)
 
 
 def padded_2(block, sides, width):
@@ -49,7 +71,7 @@
         ],
         axis=1,
     )
-    gathered = lax.all_gather(local, ("seq", "win"), axis=0, tiled=True)
+    gathered = gather_by_bits(local, ("seq", "win"), 0)
     full_rows = gathered.shape[0]
     split = blocks * taps * c2
     return [

time: 502 us -> 1020 us (2.03); the launches traced: 500 us -> 1010 us
  waiting for transfers between devices: 308 us -> 763 us
  other arithmetic: 27.4 us -> 70.8 us
    ppermute x0 -> x5, waiting for transfers between devices: none -> 576 us  [doubled(): other = lax.ppermute(tiles, axis, [(i, i ^ stride) for i in range(length)])]
    all_gather x1 -> x0, waiting for transfers between devices: 121 us -> none  [fetch_weights(): gathered = lax.all_gather(local, ('seq', 'win'), axis=0, tiled=True)]
    select_n x0 -> x4, other arithmetic: none -> 24.1 us  [doubled(): tiles = jnp.where(upper == 0, both, both[::-1]).reshape(-1, *value.shape)]
    another operation x0 -> x6, other arithmetic: none -> 20.2 us  [doubled(): both = jnp.stack([tiles, other])]
    unnamed x31 -> x42, local copies, waits for them, and re-layouts: 27.3 us -> 31.2 us
    unnamed x3 -> x2, waiting for transfers between devices: 181 us -> 181 us
  transfers between devices with their start and end apart: 10 -> 14, of which waited for: 5 -> 9; matrix products, arithmetic and copies ran while one was open for 14% -> 8% of each run, Pallas kernels for 0% -> 0%
where the time goes in v1:
time: 1020 us; the launch traced here: 1010 us
  waiting for transfers between devices  763 us (75%)
  other arithmetic  70.8 us (7%)
  local copies, waits for them, and re-layouts  63 us (6%)
  matrix products  62.5 us (6%)
  starting transfers between devices  33.7 us (3%)
  between operations  14.8 us (1%)
    ppermute x5, waiting for transfers between devices, doubled(): other = lax.ppermute(tiles, axis, [(i, i ^ stride) for i in range(length)])  576 us
    unnamed x2, waiting for transfers between devices  181 us
    unnamed x42, local copies, waits for them, and re-layouts  31.2 us
    slice x3, local copies, waits for them, and re-layouts, fetch_weights(): gathered[:, b * taps * c2:(b + 1) * taps * c2].reshape(full_rows, taps, c2)  26.9 us
    select_n x4, other arithmetic, doubled(): tiles = jnp.where(upper == 0, both, both[::-1]).reshape(-1, *value.shape)  24.1 us
  transfers between devices with their start and end apart: 14, of which 9 were waited for; matrix products, arithmetic and copies ran while one was open for 8% of the time, Pallas kernels for 0%

profile of v1, /device:TPU:0, one launch (start us, length us, event | category | flops | bytes accessed | tf_op | source)
XLA Modules:
  0.0 1007.4 jit_solution(9190054750917532734)
XLA Ops:
  8.9 1.6 collective-permute-done.1
  11.0 3.0 collective-permute-start.2
  13.9 26.3 %collective-permute-done.2 = bf16[2,48,6144]{2,1,0:T(8,128)(2,1)S(1)} collective-permute-done((bf16[2,48,6144]{2,1,0:T(8,128)(2,1)S(1)}, bf16[2,48,6144]{2,1,0:T(8,128)(2,1)S(1)}, u32[]{:S(2)}, u32[]{:S(2)}) %collective-permute-start.2) | collective-permute-done | bytes 1179680 | tf_op jit(solution)/shard_map/ppermute | solution.py:21
  40.9 1.8 collective-permute-start.3
  42.7 51.2 %collective-permute-done.3 = bf16[4,48,6144]{2,1,0:T(8,128)(2,1)} collective-permute-done((bf16[4,48,6144]{2,1,0:T(8,128)(2,1)S(1)}, bf16[4,48,6144]{2,1,0:T(8,128)(2,1)}, u32[]{:S(2)}, u32[]{:S(2)}) %collective-permute-start.3) | collective-permute-done | bytes 2359328 | tf_op jit(solution)/shard_map/ppermute | solution.py:21
  93.8 2.1 pad_maximum_fusion.3
  95.9 3.4 reverse_select_fusion.2
  99.3 1.5 collective-permute-start.4
  100.8 101.3 %collective-permute-done.4 = bf16[8,48,6144]{2,1,0:T(8,128)(2,1)} collective-permute-done((bf16[8,48,6144]{2,1,0:T(8,128)(2,1)}, bf16[8,48,6144]{2,1,0:T(8,128)(2,1)}, u32[]{:S(2)}, u32[]{:S(2)}) %collective-permute-start.4) | collective-permute-done | bytes 4718624 | tf_op jit(solution)/shard_map/ppermute | solution.py:21
  202.1 8.3 pad_maximum_fusion.2
  210.4 14.9 %reverse_select_fusion.1 = bf16[2,8,48,6144]{3,2,1,0:T(8,128)(2,1)} fusion(bf16[2,8,48,6144]{3,2,1,0:T(8,128)(2,1)} %pad_maximum_fusion.2, pred[]{:T(512)S(6)} %eq.16), kind=kLoop, calls=%fused_computation.7 | loop fusion | flops 4718592 | bytes 18874368 | tf_op jit(solution)/shard_map/jit(_where)/select_n | solution.py:24
  225.3 2.2 collective-permute-start.5
  230.8 5.1 collective-permute-start
  235.9 395.7 %collective-permute-done.5 = bf16[16,48,6144]{2,1,0:T(8,128)(2,1)} collective-permute-done((bf16[16,48,6144]{2,1,0:T(8,128)(2,1)}, bf16[16,48,6144]{2,1,0:T(8,128)(2,1)}, u32[]{:S(2)}, u32[]{:S(2)}) %collective-permute-start.5) | collective-permute-done | bytes 9437216 | tf_op jit(solution)/shard_map/ppermute | solution.py:21
  631.6 9.2 pad_maximum_fusion
  640.9 5.3 reverse_select_fusion
  646.2 6.3 fusion.127
  652.5 4.4 copy-done
  656.9 10.4 %copy.44 = bf16[1536,2304]{0,1:T(8,128)(2,1)} copy(bf16[1536,2304]{1,0:T(8,128)(2,1)} %get-tuple-element.13) | data formatting | bytes 14155776 | tf_op jit(solution)/shard_map/slice | solution.py:79
  667.3 4.5 fusion.42
  671.8 3.8 fusion.44
  675.6 10.3 %copy.48 = bf16[1536,2304]{0,1:T(8,128)(2,1)} copy(bf16[1536,2304]{1,0:T(8,128)(2,1)} %get-tuple-element.12) | data formatting | bytes 14155776 | tf_op jit(solution)/shard_map/slice | solution.py:79
  685.9 3.6 fusion.66
  689.5 3.6 multiply_convert_fusion.2
  695.7 4.7 collective-permute-start.7
  703.2 3.7 fusion.82
  706.9 3.0 fusion.2
  709.9 1.5 fusion.133
  711.4 4.2 collective-permute-start.10
  715.6 1.5 fusion.104
  717.1 1.5 fusion.103
  718.5 4.2 fusion.1
  723.8 1.5 collective-permute-start.9
  726.4 3.4 collective-permute-done.9
  729.8 2.7 fusion.38
  732.5 4.1 fusion.74
  736.6 2.9 multiply_convert_fusion.1
  743.9 4.3 fusion
  748.3 16.9 %pad_maximum_fusion.1 = bf16[1536,6144]{0,1:T(8,128)(2,1)} fusion(bf16[1536,768]{0,1:T(8,128)(2,1)} %fusion.2, bf16[1536,768]{0,1:T(8,128)(2,1)} %multiply_convert_fusion.1, bf16[1536,2304]{0,1:T(8,128)(2,1)} %fusion.1, bf16[1536,2304]{0,1:T(8,128)(2,1)} %fusion), kind=kLoop, calls=%fused_computation.2 | loop fusion | flops 75497472 | bytes 37748736 | tf_op jit(solution)/shard_map/concatenate | solution.py:163
  765.2 23.1 %copy.54 = bf16[1536,6144]{1,0:T(8,128)(2,1)} copy(bf16[1536,6144]{0,1:T(8,128)(2,1)} %pad_maximum_fusion.1) | data formatting | bytes 37748736
  789.6 4.6 fusion.7
  794.2 5.1 collective-permute-start.12
  799.2 3.0 fusion.41
  802.2 1.6 collective-permute-start.11
  803.8 2.9 fusion.43
  808.1 6.0 fusion.30
  814.0 181.4 %reduce-scatter.4.cloned.1.call-done = bf16[48,6144]{1,0:T(8,128)(2,1)} async-done(((bf16[1536,6144]{1,0:T(8,128)(2,1)}), bf16[48,6144]{1,0:T(8,128)(2,1)}) %reduce-scatter.4.cloned.1.call-update) | async-done | bytes 589840
  997.3 1.6 copy.52
  (79 shorter events, 23.7 us)
Async XLA Ops:
  7.2 1.2 copy-start.6
  7.2 988.2 %reduce-scatter.4.cloned.1.call-start = ((), (), s32[]{:S(2)}) async-start(), calls=%async_computation.1 | async-start | bytes 19464192
  8.4 2.1 collective-permute-start.1
  11.0 29.2 %collective-permute-start.2 = (bf16[2,48,6144]{2,1,0:T(8,128)(2,1)S(1)}, bf16[2,48,6144]{2,1,0:T(8,128)(2,1)S(1)}, u32[]{:S(2)}, u32[]{:S(2)}) collective-permute-start(bf16[2,48,6144]{2,1,0:T(8,128)(2,1)S(1)} %get-tuple-element.19), channel_id=1, source_target_pairs={{0,2},{1,3},{2,0},{3,1},{4,6},{5,7},{6,4},{7,5},{8,10},{9,11},{10,... | collective-permute-start | bytes 3538952 | tf_op jit(solution)/shard_map/ppermute | solution.py:21
  40.9 53.0 %collective-permute-start.3 = (bf16[4,48,6144]{2,1,0:T(8,128)(2,1)S(1)}, bf16[4,48,6144]{2,1,0:T(8,128)(2,1)}, u32[]{:S(2)}, u32[]{:S(2)}) collective-permute-start(bf16[4,48,6144]{2,1,0:T(8,128)(2,1)S(1)} %bitcast.174), channel_id=1, source_target_pairs={{0,4},{1,5},{2,6},{3,7},{4,0},{5,1},{6,2},{7,3},{8,12},{9,13},{10,... | collective-permute-start | bytes 7077896 | tf_op jit(solution)/shard_map/ppermute | solution.py:21
  99.3 102.8 %collective-permute-start.4 = (bf16[8,48,6144]{2,1,0:T(8,128)(2,1)}, bf16[8,48,6144]{2,1,0:T(8,128)(2,1)}, u32[]{:S(2)}, u32[]{:S(2)}) collective-permute-start(bf16[8,48,6144]{2,1,0:T(8,128)(2,1)} %bitcast.13), channel_id=1, source_target_pairs={{0,8},{1,9},{2,10},{3,11},{4,12},{5,13},{6,14},{7,15},{8,0},{9,1},... | collective-permute-start | bytes 14155784 | tf_op jit(solution)/shard_map/ppermute | solution.py:21
  210.4 17.0 %copy-start.7 = (f32[2,1536]{1,0:T(2,128)S(1)}, f32[2,1536]{1,0:T(2,128)}, u32[]{:S(2)}) copy-start(f32[2,1536]{1,0:T(2,128)} %param.13) | copy-start | bytes 36868
  210.4 17.0 %copy-start.8 = (f32[2,1536]{1,0:T(2,128)S(1)}, f32[2,1536]{1,0:T(2,128)}, u32[]{:S(2)}) copy-start(f32[2,1536]{1,0:T(2,128)} %param.12) | copy-start | bytes 36868
  210.4 17.1 %copy-start.4 = (bf16[1,384,1536]{2,1,0:T(8,128)(2,1)S(1)}, bf16[1,384,1536]{2,1,0:T(8,128)(2,1)}, u32[]{:S(2)}) copy-start(bf16[1,384,1536]{2,1,0:T(8,128)(2,1)} %param.8) | copy-start | bytes 3538948
  225.3 10.6 %copy-start.9 = (f32[2,768]{1,0:T(2,128)S(1)}, f32[2,768]{1,0:T(2,128)}, u32[]{:S(2)}) copy-start(f32[2,768]{1,0:T(2,128)} %param.15) | copy-start | bytes 18436
  225.3 10.6 %copy-start.10 = (f32[2,768]{1,0:T(2,128)S(1)}, f32[2,768]{1,0:T(2,128)}, u32[]{:S(2)}) copy-start(f32[2,768]{1,0:T(2,128)} %param.14) | copy-start | bytes 18436
  225.3 406.4 %collective-permute-start.5 = (bf16[16,48,6144]{2,1,0:T(8,128)(2,1)}, bf16[16,48,6144]{2,1,0:T(8,128)(2,1)}, u32[]{:S(2)}, u32[]{:S(2)}) collective-permute-start(bf16[16,48,6144]{2,1,0:T(8,128)(2,1)} %bitcast.171), channel_id=1, source_target_pairs={{0,16},{1,17},{2,18},{3,19},{4,20},{5,21},{6,22},{7,23},{8,24},{9,... | collective-permute-start | bytes 28311560 | tf_op jit(solution)/shard_map/ppermute | solution.py:21
  228.5 1.0 copy-start.1
  229.5 442.3 %collective-permute-start.6 = (bf16[8,1536]{1,0:T(8,128)(2,1)S(1)}, bf16[8,1536]{1,0:T(8,128)(2,1)S(1)}, u32[]{:S(2)}, u32[]{:S(2)}) collective-permute-start(bf16[8,1536]{1,0:T(8,128)(2,1)S(1)} %get-tuple-element.17), channel_id=1, source_target_pairs={{4,0},{8,4},{12,8},{16,12},{20,16},{24,20},{28,24},{5,1},{9,5},{13... | collective-permute-start | bytes 73736 | tf_op jit(solution)/shard_map/ppermute | solution.py:40
  230.8 455.1 %collective-permute-start = (bf16[8,1536]{1,0:T(8,128)(2,1)S(1)}, bf16[8,1536]{1,0:T(8,128)(2,1)S(1)}, u32[]{:S(2)}, u32[]{:S(2)}) collective-permute-start(bf16[8,1536]{1,0:T(8,128)(2,1)S(1)} %get-tuple-element.16), channel_id=1, source_target_pairs={{0,4},{4,8},{8,12},{12,16},{16,20},{20,24},{24,28},{1,5},{5,9},{9,... | collective-permute-start | bytes 73736 | tf_op jit(solution)/shard_map/ppermute | solution.py:37
  646.2 10.7 %copy-start = (bf16[2,16,48,6144]{3,2,1,0:T(8,128)(2,1)}, bf16[2,16,48,6144]{3,2,1,0:T(8,128)(2,1)S(1)}, u32[]{:S(2)}) copy-start(bf16[2,16,48,6144]{3,2,1,0:T(8,128)(2,1)S(1)} %reverse_select_fusion) | copy-start | bytes 56623108
  656.9 10.4 %copy-start.5 = (bf16[1,384,1536]{2,1,0:T(8,128)(2,1)S(1)}, bf16[1,384,1536]{2,1,0:T(8,128)(2,1)}, u32[]{:S(2)}) copy-start(bf16[1,384,1536]{2,1,0:T(8,128)(2,1)} %param.8) | copy-start | bytes 3538948
  667.3 4.5 copy-start.2
  685.9 8.6 slice-start
  689.5 5.0 slice-start.1
  693.2 36.6 %copy-start.14 = (f32[384,1536]{1,0:T(8,128)}, f32[384,1536]{1,0:T(8,128)S(1)}, u32[]{:S(2)}) copy-start(f32[384,1536]{1,0:T(8,128)S(1)} %get-tuple-element.25) | copy-start | bytes 7077892
  693.2 7.2 collective-permute-start.8
  695.7 6.3 collective-permute-start.7
  702.0 1.3 copy-start.11
  703.2 3.7 copy-start.15
  711.4 14.0 %collective-permute-start.10 = (bf16[16,768]{1,0:T(8,128)(2,1)S(1)}, bf16[16,768]{1,0:T(8,128)(2,1)S(1)}, u32[]{:S(2)}, u32[]{:S(2)}) collective-permute-start(bf16[16,768]{1,0:T(8,128)(2,1)S(1)} %get-tuple-element.23), channel_id=1, source_target_pairs={{0,4},{4,8},{8,12},{12,16},{16,20},{20,24},{24,28},{1,5},{5,9},{9,... | collective-permute-start | bytes 73736 | tf_op jit(solution)/shard_map/ppermute | solution.py:37
  723.8 6.0 collective-permute-start.9
  732.5 4.1 copy-start.12
  788.3 1.3 copy-start.16
  794.2 9.6 collective-permute-start.12
  802.2 5.9 copy-start.13
  802.2 5.9 collective-permute-start.11
  997.3 1.7 copy-start.3
Sparse Core Ops, SparseCore 0:
  788.5 206.8 reduce-scatter.3
